TPU v7x, 32 devices: a whole 2x2x4 slice. The times are simulated.
32 devices in a mesh: shots: 2 (over y), gx: 4 (over z), gy: 4 (over x, core).
Axes of the slice: x: 2, y: 2, z: 4, core: 2. Of those that a mesh axis runs over, the one named last changes fastest.
Arguments:
- p_now: float32 [64, 64, 128], P(('shots', 'gx'), 'gy'), parts along dimension 0, may hold values from -6 to 6
- q_now: float32 [64, 64, 128], P(('shots', 'gx'), 'gy'), parts along dimension 0, may hold values from -6 to 6
- p_prev: float32 [64, 64, 128], P(('shots', 'gx'), 'gy'), parts along dimension 0, may hold values from -6 to 6
- q_prev: float32 [64, 64, 128], P(('shots', 'gx'), 'gy'), parts along dimension 0, may hold values from -6 to 6
- speed: float32 [32, 64, 128], P('gx', 'gy'), may hold values from 0.05 to 0.2
- epsilon: float32 [32, 64, 128], P('gx', 'gy'), may hold values from 0.05 to 0.35
- delta: float32 [32, 64, 128], P('gx', 'gy'), may hold values from 0 to 0.3
- theta: float32 [32, 64, 128], P('gx', 'gy'), may hold values from -1 to 1
- phi: float32 [32, 64, 128], P('gx', 'gy'), may hold values from -3.140625 to 3.140625
- snapshots: bfloat16 [2, 64, 64, 128], P(None, ('shots', 'gx'), 'gy'), parts along dimension 1, may hold values from -6 to 6
- traces: float32 [1024, 4096], P(None, ('shots', 'gx', 'gy')), parts along dimension 1, may hold values from -6 to 6
- time_steps: int32 [4], P('shots'), parts along dimension 0, may hold values from 0 to 1023
- rec_owner: int32 [4096, 1], P(('shots', 'gx', 'gy')), parts along dimension 0, may hold values from 0 to 3; in each aligned block of 128 rows (0 to 127, 128 to 255, ...) at most 64 rows name the same one
- rec_local: int32 [4096], P(('shots', 'gx', 'gy')), parts along dimension 0, may hold values from 0 to 16383
Outputs:
- p_next: float32 [64, 64, 128], P(('shots', 'gx'), 'gy'), parts along dimension 0
- q_next: float32 [64, 64, 128], P(('shots', 'gx'), 'gy'), parts along dimension 0
- p_mid: float32 [64, 64, 128], P(('shots', 'gx'), 'gy'), parts along dimension 0
- q_mid: float32 [64, 64, 128], P(('shots', 'gx'), 'gy'), parts along dimension 0
- image: float32 [64, 64, 128], P(('shots', 'gx'), 'gy'), parts along dimension 0
There are 2 independent parts, one for each index of `shots`. A program takes and returns all parts, laid end to end along the dimension named above; an argument that names none is the same for every part. Nothing has to cross between parts.
Inputs may be any that keep to these rules, and one draw needn't show every extreme that they name: `rec_owner`: the 128 receivers of one device (aligned blocks of 128 rows) name any one owner at most 64 times, a bound that some block reaches. `rec_local`: A receiver's cell lies in the band of the second dimension that the device holding the receiver covers.
All inputs are finite; a program needn't handle non-finite values.
Results may differ from a plain program's by a relative error of at most 0.0003.
Values sent between devices are 32-bit elements; how exact they have to be, the bound alone decides.
No kernel may reach another device: no remote copies, remote signals or barrier semaphores. Data moves between devices by JAX's collectives and lax.ppermute only.
A program may use at most 64 MiB of HBM per device.

v0:
```python
import jax
import jax.numpy as jnp
from jax import lax
from jax.sharding import PartitionSpec as P

second_coef = (-205.0 / 72.0, 8.0 / 5.0, -1.0 / 5.0, 8.0 / 315.0, -1.0 / 560.0)
first_coef = (4.0 / 5.0, -1.0 / 5.0, 4.0 / 105.0, -1.0 / 280.0)


def padded_2(cells, sides, width):
    for axis, dim in sides:
        count = lax.axis_size(axis)
        ends = count - 1
        head = lax.slice_in_dim(cells, 0, width, axis=dim)
        tail = lax.slice_in_dim(cells, cells.shape[dim] - width, cells.shape[dim], axis=dim)
        cells = jnp.concatenate(
            [
                lax.ppermute(tail, axis, [(i, (i + 1) % count) for i in range(ends)]),
                cells,
                lax.ppermute(head, axis, [((i + 1) % count, i) for i in range(ends)]),
            ],
            axis=dim,
        )
    return cells


def derivatives(padded, sx, sy, sz):

    def part(dx, dy, dz):
        return padded[:, 4 + dx : 4 + dx + sx, 4 + dy : 4 + dy + sy, 4 + dz : 4 + dz + sz]

    centre = part(0, 0, 0)
    dxx = second_coef[0] * centre
    dyy = second_coef[0] * centre
    dzz = second_coef[0] * centre
    for k in range(1, 5):
        dxx = dxx + second_coef[k] * (part(k, 0, 0) + part(-k, 0, 0))
        dyy = dyy + second_coef[k] * (part(0, k, 0) + part(0, -k, 0))
        dzz = dzz + second_coef[k] * (part(0, 0, k) + part(0, 0, -k))
    dy_wide = 0.0
    dz_xwide = 0.0
    dz_ywide = 0.0
    for k in range(1, 5):
        weight = first_coef[k - 1]
        dy_wide = dy_wide + weight * (
            padded[:, :, 4 + k : 4 + k + sy, 4 : 4 + sz]
            - padded[:, :, 4 - k : 4 - k + sy, 4 : 4 + sz]
        )
        dz_xwide = dz_xwide + weight * (
            padded[:, :, 4 : 4 + sy, 4 + k : 4 + k + sz]
            - padded[:, :, 4 : 4 + sy, 4 - k : 4 - k + sz]
        )
        dz_ywide = dz_ywide + weight * (
            padded[:, 4 : 4 + sx, :, 4 + k : 4 + k + sz]
            - padded[:, 4 : 4 + sx, :, 4 - k : 4 - k + sz]
        )
    dxy = 0.0
    dxz = 0.0
    dyz = 0.0
    for k in range(1, 5):
        weight = first_coef[k - 1]
        dxy = dxy + weight * (dy_wide[:, 4 + k : 4 + k + sx] - dy_wide[:, 4 - k : 4 - k + sx])
        dxz = dxz + weight * (dz_xwide[:, 4 + k : 4 + k + sx] - dz_xwide[:, 4 - k : 4 - k + sx])
        dyz = dyz + weight * (
            dz_ywide[:, :, 4 + k : 4 + k + sy] - dz_ywide[:, :, 4 - k : 4 - k + sy]
        )
    return (centre, dxx, dyy, dzz, dxy, dxz, dyz)


def advance(padded, previous, speed, epsilon, delta, theta, phi, source):
    sx, sy, sz = (previous.shape[1], previous.shape[2], previous.shape[3])
    centre, dxx, dyy, dzz, dxy, dxz, dyz = derivatives(padded, sx, sy, sz)
    axis_x = jnp.sin(theta) * jnp.cos(phi)
    axis_y = jnp.sin(theta) * jnp.sin(phi)
    axis_z = jnp.cos(theta)
    rotated = (
        axis_x * axis_x * dxx
        + axis_y * axis_y * dyy
        + axis_z * axis_z * dzz
        + 2.0 * axis_x * axis_y * dxy
        + 2.0 * axis_x * axis_z * dxz
        + 2.0 * axis_y * axis_z * dyz
    )
    remainder = dxx + dyy + dzz - rotated
    root_delta = jnp.sqrt(1.0 + 2.0 * delta)
    p_new = (
        2.0 * centre[0]
        - previous[0]
        + speed * ((1.0 + 2.0 * epsilon) * remainder[0] + root_delta * rotated[1])
        + source
    )
    q_new = (
        2.0 * centre[1] - previous[1] + speed * (root_delta * remainder[0] + rotated[1]) + source
    )
    return jnp.stack([p_new, q_new])


def pad_depth(fields):
    return jnp.pad(fields, ((0, 0), (0, 0), (0, 0), (4, 4)))


def widened(fields):
    return pad_depth(padded_2(fields, (("gx", 1), ("gy", 2)), 4))


def local(
    p_now,
    q_now,
    p_prev,
    q_prev,
    speed,
    epsilon,
    delta,
    theta,
    phi,
    snapshots,
    traces,
    time_steps,
    rec_owner,
    rec_local,
):
    sx, sy, sz = p_now.shape
    cells = sx * sy * sz
    groups = lax.axis_size("gx")
    held = rec_local.shape[0]
    samples = jnp.take(traces, time_steps, axis=0)
    owner = rec_owner[:, 0]
    capacity = 2 * held // groups
    onehot = (owner[:, None] == jnp.arange(groups, dtype=jnp.int32)[None, :]).astype(jnp.int32)
    running = jnp.cumsum(onehot, axis=0)
    rank = jnp.sum(onehot * running, axis=1) - 1
    position = owner * capacity + rank
    payload = jnp.concatenate([samples, rec_local.astype(jnp.float32)[None, :]], axis=0)
    slots = jnp.zeros((3, groups * capacity), jnp.float32).at[:, position].set(payload)
    slots = slots.reshape(3, groups, capacity)
    arrived = lax.all_to_all(slots, "gx", split_axis=1, concat_axis=1, tiled=True)
    values = arrived[0:2].reshape(2, groups * capacity)
    target = arrived[2].reshape(groups * capacity).astype(jnp.int32)
    sources = jnp.zeros((2, cells), jnp.float32).at[:, target].add(values).reshape(2, sx, sy, sz)
    current = jnp.stack([p_now, q_now])
    earlier = jnp.stack([p_prev, q_prev])
    middle = advance(widened(current), earlier, speed, epsilon, delta, theta, phi, sources[0])
    final = advance(widened(middle), current, speed, epsilon, delta, theta, phi, sources[1])
    image = (
        snapshots[0].astype(jnp.float32) * middle[0] + snapshots[1].astype(jnp.float32) * final[0]
    )
    return (final[0], final[1], middle[0], middle[1], image)


def solution(mesh):
    return jax.shard_map(
        local,
        mesh=mesh,
        in_specs=(
            P(("shots", "gx"), "gy", None),
            P(("shots", "gx"), "gy", None),
            P(("shots", "gx"), "gy", None),
            P(("shots", "gx"), "gy", None),
            P("gx", "gy", None),
            P("gx", "gy", None),
            P("gx", "gy", None),
            P("gx", "gy", None),
            P("gx", "gy", None),
            P(None, ("shots", "gx"), "gy", None),
            P(None, ("shots", "gx", "gy")),
            P("shots"),
            P(("shots", "gx", "gy"), None),
            P(("shots", "gx", "gy")),
        ),
        out_specs=(
            P(("shots", "gx"), "gy", None),
            P(("shots", "gx"), "gy", None),
            P(("shots", "gx"), "gy", None),
            P(("shots", "gx"), "gy", None),
            P(("shots", "gx"), "gy", None),
        ),
        check_vma=False,
    )
```

profile of v0, /device:TPU:18, one launch (start us, length us, event | category | flops | bytes accessed | tf_op | source)
XLA Modules:
  0.0 71.5 jit_solution(5272176775762559091)
XLA Ops:
  0.6 0.7 %compare_select_fusion.1 = s32[2]{0:T(128)S(1)} fusion(s32[2]{0:T(128)} %param.25), kind=kLoop, calls=%fused_computation.299 | loop fusion | flops 6 | bytes 16 | tf_op jit(solution)/shard_map/jit(_take)/jit(_where)/select_n | solution.py:126
  1.4 0.7 compare_and_fusion
  2.0 0.7 %fusion.156 = s32[128,4]{1,0:T(8,128)S(1)} fusion(s32[128]{0:T(128)} %bitcast.80), kind=kLoop, calls=%fused_computation.286 | loop fusion | flops 1024 | bytes 2560 | tf_op jit(solution)/shard_map/convert_element_type | solution.py:129
  2.9 0.8 %select_reduce_fusion = s32[128]{0:T(128)S(1)} fusion(s32[128,4]{1,0:T(8,128)S(1)} %reduce_window_sum.11, s32[128]{0:T(128)} %bitcast.81), kind=kLoop, calls=%fused_computation.284 | loop fusion | flops 1408 | bytes 3072 | tf_op jit(solution)/shard_map/reduce_sum | solution.py:131
  3.8 0.7 fusion.160
  4.4 0.7 convert_bitcast_fusion
  5.1 0.6 gather_fusion
  5.9 0.9 %scatter_custom_fusion = f32[3,256]{0,1:T(8,128)S(1)} fusion(s32[128]{0:T(128)S(1)} %fusion.160, f32[128,3]{1,0:T(8,128)S(1)} %copy.25, f32[]{:T(128)} %constant.26.clone.1), kind=kCustom, calls=%fused_computation.287 | custom fusion | bytes 3076 | tf_op jit(solution)/shard_map/scatter | solution.py:134
  6.9 0.7 reshape.111
  7.6 5.2 %all-to-all-start = ((f32[4,1,192]{2,1,0:T(1,128)}), f32[4,1,192]{2,1,0:T(1,128)S(1)}, u32[]{:S(2)}, u32[]{:S(2)}) async-start(f32[4,1,192]{2,1,0:T(1,128)} %reshape.111), calls=%async_computation | async-start | bytes 8192 | tf_op jit(solution)/shard_map/all_to_all | solution.py:136
  12.8 0.8 %fusion.152 = (f32[2,4,16,128]{3,2,1,0:T(8,128)S(1)}, f32[2,4,16,128]{3,2,1,0:T(8,128)S(1)}) fusion(f32[1,8,16,128]{3,2,1,0:T(8,128)} %bitcast.59, f32[1,8,16,128]{3,2,1,0:T(8,128)} %bitcast.47), kind=kLoop, calls=%fused_computation.259 | loop fusion | flops 32768 | bytes 262144 | tf_op jit(solution)/shard_map/stack | solution.py:140
  13.6 2.5 %collective-permute-start = (f32[2,4,16,128]{3,2,1,0:T(8,128)S(1)}, f32[2,4,16,128]{3,2,1,0:T(8,128)S(1)}, u32[]{:S(2)}, u32[]{:S(2)}) collective-permute-start(f32[2,4,16,128]{3,2,1,0:T(8,128)S(1)} %get-tuple-element.42), channel_id=1, source_target_pairs={{4,0},{8,4},{12,8},{5,1},{9,5},{13,9},{6,2},{10,6},{14,10},{7,3},{... | collective-permute-start | bytes 196616 | tf_op jit(solution)/shard_map/ppermute | solution.py:20
  16.1 3.4 %collective-permute-start.1 = (f32[2,4,16,128]{3,2,1,0:T(8,128)S(1)}, f32[2,4,16,128]{3,2,1,0:T(8,128)S(1)}, u32[]{:S(2)}, u32[]{:S(2)}) collective-permute-start(f32[2,4,16,128]{3,2,1,0:T(8,128)S(1)} %get-tuple-element.41), channel_id=1, source_target_pairs={{0,4},{4,8},{8,12},{1,5},{5,9},{9,13},{2,6},{6,10},{10,14},{3,7},{... | collective-permute-start | bytes 196616 | tf_op jit(solution)/shard_map/ppermute | solution.py:18
  19.4 1.1 %fusion.171 = (f32[8,16,128]{2,1,0:T(8,128)S(1)}, f32[8,16,128]{2,1,0:T(8,128)S(1)}) fusion(f32[8,16,128]{2,1,0:T(8,128)} %param.21), kind=kLoop, calls=%fused_computation.311 | loop fusion | bytes 196608 | tf_op jit(solution)/shard_map/sin | solution.py:73
  20.5 1.1 %fusion.161 = (f32[8,16,128]{2,1,0:T(8,128)S(1)}, f32[8,16,128]{2,1,0:T(8,128)S(1)}, f32[8,16,128]{2,1,0:T(8,128)S(1)}, f32[8,16,128]{2,1,0:T(8,128)S(1)}, f32[8...) fusion(f32[8,16,128]{2,1,0:T(8,128)S(1)} %get-tuple-element.44, f32[8,16,128]{2,1,0:T(8,128)} %param.22, ...), kind=kLoop, calls=%fused_computation.309 | loop fusion | flops 163840 | bytes 589824 | tf_op jit(solution)/shard_map/mul | solution.py:77
  22.2 0.7 reduce.8
  23.3 5.1 %scatter_custom_fusion.1 = f32[2,16384]{0,1:T(8,128)} fusion(s32[256]{0:T(256)S(1)} %bitcast.82, f32[256,2]{1,0:T(8,128)S(1)} %copy.28, f32[]{:T(128)} %constant.26.clone.1), kind=kCustom, calls=%fused_computation.5 | custom fusion | flops 512 | bytes 131076 | tf_op jit(solution)/shard_map/scatter-add | solution.py:139
  28.4 12.3 %slice_reduce_fusion.1 = (f32[16384]{0:T(1024)S(1)}, f32[16384]{0:T(1024)S(1)}) fusion(f32[2,16384]{0,1:T(8,128)} %scatter_custom_fusion.1), kind=kLoop, calls=%fused_computation.4 | loop fusion | bytes 262144 | tf_op jit(solution)/shard_map/slice | solution.py:142
  40.8 1.9 %collective-permute-start.2 = (f32[2,16,4,128]{3,2,1,0:T(4,128)S(1)}, f32[2,16,4,128]{3,2,1,0:T(4,128)S(1)}, u32[]{:S(2)}, u32[]{:S(2)}) collective-permute-start(f32[2,16,4,128]{3,2,1,0:T(4,128)S(1)} %get-tuple-element.27), channel_id=1, source_target_pairs={{1,0},{2,1},{3,2},{5,4},{6,5},{7,6},{9,8},{10,9},{11,10},{13,12},{... | collective-permute-start | bytes 196616 | tf_op jit(solution)/shard_map/ppermute | solution.py:20
  42.8 2.5 %collective-permute-start.3 = (f32[2,16,4,128]{3,2,1,0:T(4,128)S(1)}, f32[2,16,4,128]{3,2,1,0:T(4,128)S(1)}, u32[]{:S(2)}, u32[]{:S(2)}) collective-permute-start(f32[2,16,4,128]{3,2,1,0:T(4,128)S(1)} %get-tuple-element.26), channel_id=1, source_target_pairs={{0,1},{1,2},{2,3},{4,5},{5,6},{6,7},{8,9},{9,10},{10,11},{12,13},{... | collective-permute-start | bytes 196616 | tf_op jit(solution)/shard_map/ppermute | solution.py:18
  45.4 3.1 %collective-permute-done.3 = f32[2,16,4,128]{3,2,1,0:T(4,128)S(1)} collective-permute-done((f32[2,16,4,128]{3,2,1,0:T(4,128)S(1)}, f32[2,16,4,128]{3,2,1,0:T(4,128)S(1)}, u32[]{:S(2)}, u32[]{:S(2)}) %collective-permute-start.3) | collective-permute-done | bytes 65568 | tf_op jit(solution)/shard_map/ppermute | solution.py:18
  49.4 0.7 fusion.18
  50.1 0.6 fusion.101
  50.9 3.1 %collective-permute-start.4 = (f32[2,4,16,128]{3,2,1,0:T(8,128)S(1)}, f32[2,4,16,128]{3,2,1,0:T(8,128)S(1)}, u32[]{:S(2)}, u32[]{:S(2)}) collective-permute-start(f32[2,4,16,128]{3,2,1,0:T(8,128)S(1)} %get-tuple-element.33), channel_id=1, source_target_pairs={{4,0},{8,4},{12,8},{5,1},{9,5},{13,9},{6,2},{10,6},{14,10},{7,3},{... | collective-permute-start | bytes 196616 | tf_op jit(solution)/shard_map/ppermute | solution.py:20
  54.0 2.7 %collective-permute-start.5 = (f32[2,4,16,128]{3,2,1,0:T(8,128)S(1)}, f32[2,4,16,128]{3,2,1,0:T(8,128)S(1)}, u32[]{:S(2)}, u32[]{:S(2)}) collective-permute-start(f32[2,4,16,128]{3,2,1,0:T(8,128)S(1)} %get-tuple-element.32), channel_id=1, source_target_pairs={{0,4},{4,8},{8,12},{1,5},{5,9},{9,13},{2,6},{6,10},{10,14},{3,7},{... | collective-permute-start | bytes 196616 | tf_op jit(solution)/shard_map/ppermute | solution.py:18
  57.0 3.1 %collective-permute-done.5 = f32[2,4,16,128]{3,2,1,0:T(8,128)S(1)} collective-permute-done((f32[2,4,16,128]{3,2,1,0:T(8,128)S(1)}, f32[2,4,16,128]{3,2,1,0:T(8,128)S(1)}, u32[]{:S(2)}, u32[]{:S(2)}) %collective-permute-start.5) | collective-permute-done | bytes 65568 | tf_op jit(solution)/shard_map/ppermute | solution.py:18
  60.2 1.9 %collective-permute-start.6 = (f32[2,16,4,128]{3,2,1,0:T(4,128)S(1)}, f32[2,16,4,128]{3,2,1,0:T(4,128)S(1)}, u32[]{:S(2)}, u32[]{:S(2)}) collective-permute-start(f32[2,16,4,128]{3,2,1,0:T(4,128)S(1)} %get-tuple-element.23), channel_id=1, source_target_pairs={{1,0},{2,1},{3,2},{5,4},{6,5},{7,6},{9,8},{10,9},{11,10},{13,12},{... | collective-permute-start | bytes 196616 | tf_op jit(solution)/shard_map/ppermute | solution.py:20
  62.1 2.5 %collective-permute-start.7 = (f32[2,16,4,128]{3,2,1,0:T(4,128)S(1)}, f32[2,16,4,128]{3,2,1,0:T(4,128)S(1)}, u32[]{:S(2)}, u32[]{:S(2)}) collective-permute-start(f32[2,16,4,128]{3,2,1,0:T(4,128)S(1)} %get-tuple-element.22), channel_id=1, source_target_pairs={{0,1},{1,2},{2,3},{4,5},{5,6},{6,7},{8,9},{9,10},{10,11},{12,13},{... | collective-permute-start | bytes 196616 | tf_op jit(solution)/shard_map/ppermute | solution.py:18
  64.7 3.1 %collective-permute-done.7 = f32[2,16,4,128]{3,2,1,0:T(4,128)S(1)} collective-permute-done((f32[2,16,4,128]{3,2,1,0:T(4,128)S(1)}, f32[2,16,4,128]{3,2,1,0:T(4,128)S(1)}, u32[]{:S(2)}, u32[]{:S(2)}) %collective-permute-start.7) | collective-permute-done | bytes 65568 | tf_op jit(solution)/shard_map/ppermute | solution.py:18
  69.5 0.6 fusion.50
  70.1 0.7 %fusion.155 = (f32[8,16,128]{2,1,0:T(8,128)}, f32[8,16,128]{2,1,0:T(8,128)}, f32[8,16,128]{2,1,0:T(8,128)S(1)}) fusion(f32[8,16,128]{2,1,0:T(8,128)S(1)} %add_add_fusion.3, bf16[2,8,16,128]{3,2,1,0:T(8,128)(2,1)S(1)} %copy-done.10, f32[8,16,128]{2,1,0:T(8,128)S(1)} %bitcast.73, f32[8,16,128]{2,1,0:T(8,128)S(1)} %copy-done.5, ...), kind=kLoop, calls=%fused_computation.279 | loop fusion | flops 327680 | bytes 983040 | tf_op jit(solution)/shard_map/add | solution.py:145
  70.8 0.7 add_add_fusion
  (58 shorter events, 4.6 us)
Async XLA Ops:
  0.6 4.5 %copy-start = (f32[1024,128]{1,0:T(8,128)S(1)}, f32[1024,128]{1,0:T(8,128)}, u32[]{:S(2)}) copy-start(f32[1024,128]{1,0:T(8,128)} %param.24) | copy-start | bytes 1572868
  7.6 14.1 %all-to-all-start = ((f32[4,1,192]{2,1,0:T(1,128)}), f32[4,1,192]{2,1,0:T(1,128)S(1)}, u32[]{:S(2)}, u32[]{:S(2)}) async-start(f32[4,1,192]{2,1,0:T(1,128)} %reshape.111), calls=%async_computation | async-start | bytes 8192 | tf_op jit(solution)/shard_map/all_to_all | solution.py:136
  13.6 27.1 %collective-permute-start = (f32[2,4,16,128]{3,2,1,0:T(8,128)S(1)}, f32[2,4,16,128]{3,2,1,0:T(8,128)S(1)}, u32[]{:S(2)}, u32[]{:S(2)}) collective-permute-start(f32[2,4,16,128]{3,2,1,0:T(8,128)S(1)} %get-tuple-element.42), channel_id=1, source_target_pairs={{4,0},{8,4},{12,8},{5,1},{9,5},{13,9},{6,2},{10,6},{14,10},{7,3},{... | collective-permute-start | bytes 196616 | tf_op jit(solution)/shard_map/ppermute | solution.py:20
  16.1 24.7 %collective-permute-start.1 = (f32[2,4,16,128]{3,2,1,0:T(8,128)S(1)}, f32[2,4,16,128]{3,2,1,0:T(8,128)S(1)}, u32[]{:S(2)}, u32[]{:S(2)}) collective-permute-start(f32[2,4,16,128]{3,2,1,0:T(8,128)S(1)} %get-tuple-element.41), channel_id=1, source_target_pairs={{0,4},{4,8},{8,12},{1,5},{5,9},{9,13},{2,6},{6,10},{10,14},{3,7},{... | collective-permute-start | bytes 196616 | tf_op jit(solution)/shard_map/ppermute | solution.py:18
  28.4 12.3 %copy-start.1 = (f32[8,16,128]{2,1,0:T(8,128)S(1)}, f32[8,16,128]{2,1,0:T(8,128)}, u32[]{:S(2)}) copy-start(f32[8,16,128]{2,1,0:T(8,128)} %param.15) | copy-start | bytes 196612
  28.4 12.3 %copy-start.3 = (f32[8,16,128]{2,1,0:T(8,128)S(1)}, f32[8,16,128]{2,1,0:T(8,128)}, u32[]{:S(2)}) copy-start(f32[8,16,128]{2,1,0:T(8,128)} %param.14) | copy-start | bytes 196612
  40.8 4.6 %collective-permute-start.2 = (f32[2,16,4,128]{3,2,1,0:T(4,128)S(1)}, f32[2,16,4,128]{3,2,1,0:T(4,128)S(1)}, u32[]{:S(2)}, u32[]{:S(2)}) collective-permute-start(f32[2,16,4,128]{3,2,1,0:T(4,128)S(1)} %get-tuple-element.27), channel_id=1, source_target_pairs={{1,0},{2,1},{3,2},{5,4},{6,5},{7,6},{9,8},{10,9},{11,10},{13,12},{... | collective-permute-start | bytes 196616 | tf_op jit(solution)/shard_map/ppermute | solution.py:20
  42.7 7.9 %copy-start.5 = (f32[8,16,128]{2,1,0:T(8,128)S(1)}, f32[8,16,128]{2,1,0:T(8,128)}, u32[]{:S(2)}) copy-start(f32[8,16,128]{2,1,0:T(8,128)} %param.18) | copy-start | bytes 196612
  42.7 7.9 %copy-start.6 = (f32[8,16,128]{2,1,0:T(8,128)S(1)}, f32[8,16,128]{2,1,0:T(8,128)}, u32[]{:S(2)}) copy-start(f32[8,16,128]{2,1,0:T(8,128)} %param.20) | copy-start | bytes 196612
  42.7 7.9 %copy-start.8 = (f32[8,16,128]{2,1,0:T(8,128)S(1)}, f32[8,16,128]{2,1,0:T(8,128)}, u32[]{:S(2)}) copy-start(f32[8,16,128]{2,1,0:T(8,128)} %param.17) | copy-start | bytes 196612
  42.8 5.7 %collective-permute-start.3 = (f32[2,16,4,128]{3,2,1,0:T(4,128)S(1)}, f32[2,16,4,128]{3,2,1,0:T(4,128)S(1)}, u32[]{:S(2)}, u32[]{:S(2)}) collective-permute-start(f32[2,16,4,128]{3,2,1,0:T(4,128)S(1)} %get-tuple-element.26), channel_id=1, source_target_pairs={{0,1},{1,2},{2,3},{4,5},{5,6},{6,7},{8,9},{9,10},{10,11},{12,13},{... | collective-permute-start | bytes 196616 | tf_op jit(solution)/shard_map/ppermute | solution.py:18
  45.3 5.4 %copy-start.7 = (f32[8,16,128]{2,1,0:T(8,128)S(1)}, f32[8,16,128]{2,1,0:T(8,128)}, u32[]{:S(2)}) copy-start(f32[8,16,128]{2,1,0:T(8,128)} %param.19) | copy-start | bytes 196612
  45.4 5.4 %copy-start.9 = (f32[8,16,128]{2,1,0:T(8,128)S(1)}, f32[8,16,128]{2,1,0:T(8,128)}, u32[]{:S(2)}) copy-start(f32[8,16,128]{2,1,0:T(8,128)} %param.16) | copy-start | bytes 196612
  50.7 20.1 %copy-start.2 = (f32[8,16,128]{2,1,0:T(8,128)}, f32[8,16,128]{2,1,0:T(8,128)S(1)}, u32[]{:S(2)}) copy-start(f32[8,16,128]{2,1,0:T(8,128)S(1)} %get-tuple-element.14) | copy-start | bytes 196612
  50.8 19.2 %copy-start.4 = (f32[8,16,128]{2,1,0:T(8,128)}, f32[8,16,128]{2,1,0:T(8,128)S(1)}, u32[]{:S(2)}) copy-start(f32[8,16,128]{2,1,0:T(8,128)S(1)} %add_add_fusion.3) | copy-start | bytes 196612
  50.9 6.2 %collective-permute-start.4 = (f32[2,4,16,128]{3,2,1,0:T(8,128)S(1)}, f32[2,4,16,128]{3,2,1,0:T(8,128)S(1)}, u32[]{:S(2)}, u32[]{:S(2)}) collective-permute-start(f32[2,4,16,128]{3,2,1,0:T(8,128)S(1)} %get-tuple-element.33), channel_id=1, source_target_pairs={{4,0},{8,4},{12,8},{5,1},{9,5},{13,9},{6,2},{10,6},{14,10},{7,3},{... | collective-permute-start | bytes 196616 | tf_op jit(solution)/shard_map/ppermute | solution.py:20
  54.0 6.2 %collective-permute-start.5 = (f32[2,4,16,128]{3,2,1,0:T(8,128)S(1)}, f32[2,4,16,128]{3,2,1,0:T(8,128)S(1)}, u32[]{:S(2)}, u32[]{:S(2)}) collective-permute-start(f32[2,4,16,128]{3,2,1,0:T(8,128)S(1)} %get-tuple-element.32), channel_id=1, source_target_pairs={{0,4},{4,8},{8,12},{1,5},{5,9},{9,13},{2,6},{6,10},{10,14},{3,7},{... | collective-permute-start | bytes 196616 | tf_op jit(solution)/shard_map/ppermute | solution.py:18
  60.2 4.5 %collective-permute-start.6 = (f32[2,16,4,128]{3,2,1,0:T(4,128)S(1)}, f32[2,16,4,128]{3,2,1,0:T(4,128)S(1)}, u32[]{:S(2)}, u32[]{:S(2)}) collective-permute-start(f32[2,16,4,128]{3,2,1,0:T(4,128)S(1)} %get-tuple-element.23), channel_id=1, source_target_pairs={{1,0},{2,1},{3,2},{5,4},{6,5},{7,6},{9,8},{10,9},{11,10},{13,12},{... | collective-permute-start | bytes 196616 | tf_op jit(solution)/shard_map/ppermute | solution.py:20
  62.1 8.0 %copy-start.10 = (bf16[2,8,16,128]{3,2,1,0:T(8,128)(2,1)S(1)}, bf16[2,8,16,128]{3,2,1,0:T(8,128)(2,1)}, u32[]{:S(2)}) copy-start(bf16[2,8,16,128]{3,2,1,0:T(8,128)(2,1)} %param.23) | copy-start | bytes 196612
  62.1 5.7 %collective-permute-start.7 = (f32[2,16,4,128]{3,2,1,0:T(4,128)S(1)}, f32[2,16,4,128]{3,2,1,0:T(4,128)S(1)}, u32[]{:S(2)}, u32[]{:S(2)}) collective-permute-start(f32[2,16,4,128]{3,2,1,0:T(4,128)S(1)} %get-tuple-element.22), channel_id=1, source_target_pairs={{0,1},{1,2},{2,3},{4,5},{5,6},{6,7},{8,9},{9,10},{10,11},{12,13},{... | collective-permute-start | bytes 196616 | tf_op jit(solution)/shard_map/ppermute | solution.py:18
where the time goes:
time: 72.1 us; the launch traced here: 71.5 us
  starting transfers between devices  25.8 us (36%)
  other arithmetic  18.3 us (25%)
  local copies, waits for them, and re-layouts  16.7 us (23%)
  waiting for transfers between devices  9.66 us (13%)
  between operations  1.04 us (1%)
    slice x1, local copies, waits for them, and re-layouts, local(): sources[0]  12.3 us
    ppermute x4, starting transfers between devices, padded_2(): lax.ppermute(tail, axis, [(i, (i + 1) % count) for i in range(ends)])  11.2 us
    ppermute x4, starting transfers between devices, padded_2(): lax.ppermute(head, axis, [((i + 1) % count, i) for i in range(ends)])  9.42 us
    ppermute x4, waiting for transfers between devices, padded_2(): lax.ppermute(tail, axis, [(i, (i + 1) % count) for i in range(ends)])  9.35 us
    all_to_all x1, starting transfers between devices, local(): lax.all_to_all(slots, 'gx', split_axis=1, concat_axis=1, tiled=True)  5.2 us
    scatter-add x1, other arithmetic, local(): jnp.zeros((2, cells), jnp.float32).at[:, target].add(values)  5.14 us
  transfers between devices with their start and end apart: 9, of which 4 were waited for; matrix products, arithmetic and copies ran while one was open for 31% of the time, Pallas kernels for 0%

commit v1 on v0

--- a/solution.py
+++ b/solution.py
@@ -133,7 +133,19 @@
     payload = jnp.concatenate([samples, rec_local.astype(jnp.float32)[None, :]], axis=0)
     slots = jnp.zeros((3, groups * capacity), jnp.float32).at[:, position].set(payload)
     slots = slots.reshape(3, groups, capacity)
-    arrived = lax.all_to_all(slots, "gx", split_axis=1, concat_axis=1, tiled=True)
+    ways, here = (lax.axis_size("gx"), lax.axis_index("gx"))
+    width_2 = slots.shape[1] // ways
+    shape = list(slots.shape)
+    shape[1] = width_2
+    height = shape[1]
+    shape[1] = height * ways
+    full = jnp.zeros(shape, slots.dtype)
+    for mask in range(ways):
+        part_2 = lax.dynamic_slice_in_dim(slots, (here ^ mask) * width_2, width_2, axis=1)
+        if mask:
+            part_2 = lax.ppermute(part_2, "gx", [(d, d ^ mask) for d in range(ways)])
+        full = lax.dynamic_update_slice_in_dim(full, part_2, (here ^ mask) * height, axis=1)
+    arrived = full
     values = arrived[0:2].reshape(2, groups * capacity)
     target = arrived[2].reshape(groups * capacity).astype(jnp.int32)
     sources = jnp.zeros((2, cells), jnp.float32).at[:, target].add(values).reshape(2, sx, sy, sz)

time: 72.1 us -> 69.6 us (0.965)
  the two profiles are of different devices: /device:TPU:18 before, /device:TPU:10 now
where the time goes in v1:
time: 69.6 us; the launch traced here: 69 us
  starting transfers between devices  24.1 us (35%)
  other arithmetic  18.3 us (26%)
  local copies, waits for them, and re-layouts  15.7 us (23%)
  waiting for transfers between devices  9.83 us (14%)
  between operations  1.06 us (2%)
    slice x1, local copies, waits for them, and re-layouts, local(): sources[0]  12.3 us
    ppermute x4, starting transfers between devices, padded_2(): lax.ppermute(head, axis, [((i + 1) % count, i) for i in range(ends)])  10.4 us
    ppermute x4, starting transfers between devices, padded_2(): lax.ppermute(tail, axis, [(i, (i + 1) % count) for i in range(ends)])  10.2 us
    ppermute x4, waiting for transfers between devices, padded_2(): lax.ppermute(tail, axis, [(i, (i + 1) % count) for i in range(ends)])  9.52 us
    scatter-add x1, other arithmetic, local(): jnp.zeros((2, cells), jnp.float32).at[:, target].add(values)  5.81 us
    ppermute x3, starting transfers between devices, local(): part_2 = lax.ppermute(part_2, 'gx', [(d, d ^ mask) for d in range(ways)])  3.52 us
  transfers between devices with their start and end apart: 11, of which 4 were waited for; matrix products, arithmetic and copies ran while one was open for 32% of the time, Pallas kernels for 0%

profile of v1, /device:TPU:10, one launch (start us, length us, event | category | flops | bytes accessed | tf_op | source)
XLA Modules:
  0.0 69.0 jit_solution(16116015259104014786)
XLA Ops:
  0.6 0.7 %compare_select_fusion.1 = s32[2]{0:T(128)S(1)} fusion(s32[2]{0:T(128)} %param.25), kind=kLoop, calls=%fused_computation.299 | loop fusion | flops 6 | bytes 16 | tf_op jit(solution)/shard_map/jit(_take)/jit(_where)/select_n | solution.py:126
  1.4 0.7 compare_and_fusion
  2.0 0.7 %fusion.156 = s32[128,4]{1,0:T(8,128)S(1)} fusion(s32[128]{0:T(128)} %bitcast.77), kind=kLoop, calls=%fused_computation.286 | loop fusion | flops 1024 | bytes 2560 | tf_op jit(solution)/shard_map/convert_element_type | solution.py:129
  2.9 0.8 %select_reduce_fusion = s32[128]{0:T(128)S(1)} fusion(s32[128,4]{1,0:T(8,128)S(1)} %reduce_window_sum.11, s32[128]{0:T(128)} %bitcast.78), kind=kLoop, calls=%fused_computation.284 | loop fusion | flops 1408 | bytes 3072 | tf_op jit(solution)/shard_map/reduce_sum | solution.py:131
  3.8 0.7 fusion.159
  4.4 0.7 convert_bitcast_fusion
  5.1 0.6 gather_fusion
  5.9 0.9 %scatter_custom_fusion = f32[3,256]{0,1:T(8,128)S(1)} fusion(s32[128]{0:T(128)S(1)} %fusion.159, f32[128,3]{1,0:T(8,128)S(1)} %copy.20, f32[]{:T(128)} %constant.32.clone.1), kind=kCustom, calls=%fused_computation.287 | custom fusion | bytes 3076 | tf_op jit(solution)/shard_map/scatter | solution.py:134
  6.9 0.5 collective-permute-start.4
  7.4 2.6 %collective-permute-start.5 = (f32[3,1,64]{2,1,0:T(1,128)S(1)}, f32[3,1,64]{2,1,0:T(1,128)S(1)}, u32[]{:S(2)}, u32[]{:S(2)}) collective-permute-start(f32[3,1,64]{2,1,0:T(1,128)S(1)} %copy.29), channel_id=1, source_target_pairs={{0,8},{4,12},{8,0},{12,4},{1,9},{5,13},{9,1},{13,5},{2,10},{6,14},... | collective-permute-start | bytes 2312 | tf_op jit(solution)/shard_map/ppermute | solution.py:146
  10.6 0.8 %fusion.152 = (f32[2,4,16,128]{3,2,1,0:T(8,128)S(1)}, f32[2,4,16,128]{3,2,1,0:T(8,128)S(1)}) fusion(f32[1,8,16,128]{3,2,1,0:T(8,128)} %bitcast.59, f32[1,8,16,128]{3,2,1,0:T(8,128)} %bitcast.47), kind=kLoop, calls=%fused_computation.259 | loop fusion | flops 32768 | bytes 262144 | tf_op jit(solution)/shard_map/stack | solution.py:152
  11.4 3.3 %collective-permute-start = (f32[2,4,16,128]{3,2,1,0:T(8,128)S(1)}, f32[2,4,16,128]{3,2,1,0:T(8,128)S(1)}, u32[]{:S(2)}, u32[]{:S(2)}) collective-permute-start(f32[2,4,16,128]{3,2,1,0:T(8,128)S(1)} %get-tuple-element.42), channel_id=1, source_target_pairs={{4,0},{8,4},{12,8},{5,1},{9,5},{13,9},{6,2},{10,6},{14,10},{7,3},{... | collective-permute-start | bytes 196616 | tf_op jit(solution)/shard_map/ppermute | solution.py:20
  14.6 2.6 %collective-permute-start.1 = (f32[2,4,16,128]{3,2,1,0:T(8,128)S(1)}, f32[2,4,16,128]{3,2,1,0:T(8,128)S(1)}, u32[]{:S(2)}, u32[]{:S(2)}) collective-permute-start(f32[2,4,16,128]{3,2,1,0:T(8,128)S(1)} %get-tuple-element.41), channel_id=1, source_target_pairs={{0,4},{4,8},{8,12},{1,5},{5,9},{9,13},{2,6},{6,10},{10,14},{3,7},{... | collective-permute-start | bytes 196616 | tf_op jit(solution)/shard_map/ppermute | solution.py:18
  17.2 1.1 %fusion.170 = (f32[8,16,128]{2,1,0:T(8,128)S(1)}, f32[8,16,128]{2,1,0:T(8,128)S(1)}) fusion(f32[8,16,128]{2,1,0:T(8,128)} %param.21), kind=kLoop, calls=%fused_computation.314 | loop fusion | bytes 196608 | tf_op jit(solution)/shard_map/sin | solution.py:73
  18.3 1.1 %fusion.160 = (f32[8,16,128]{2,1,0:T(8,128)S(1)}, f32[8,16,128]{2,1,0:T(8,128)S(1)}, f32[8,16,128]{2,1,0:T(8,128)S(1)}, f32[8,16,128]{2,1,0:T(8,128)S(1)}, f32[8...) fusion(f32[8,16,128]{2,1,0:T(8,128)S(1)} %get-tuple-element.48, f32[8,16,128]{2,1,0:T(8,128)} %param.22, ...), kind=kLoop, calls=%fused_computation.312 | loop fusion | flops 163840 | bytes 589824 | tf_op jit(solution)/shard_map/mul | solution.py:77
  19.9 5.8 %scatter_custom_fusion.1 = f32[2,16384]{0,1:T(8,128)} fusion(s32[256]{0:T(256)S(1)} %bitcast.79, f32[256,2]{1,0:T(8,128)S(1)} %bitcast.76, f32[]{:T(128)} %constant.32.clone.1), kind=kCustom, calls=%fused_computation.5 | custom fusion | flops 512 | bytes 131076 | tf_op jit(solution)/shard_map/scatter-add | solution.py:151
  25.7 12.3 %slice_reduce_fusion.1 = (f32[16384]{0:T(1024)S(1)}, f32[16384]{0:T(1024)S(1)}) fusion(f32[2,16384]{0,1:T(8,128)} %scatter_custom_fusion.1), kind=kLoop, calls=%fused_computation.4 | loop fusion | bytes 262144 | tf_op jit(solution)/shard_map/slice | solution.py:154
  38.1 1.9 %collective-permute-start.2 = (f32[2,16,4,128]{3,2,1,0:T(4,128)S(1)}, f32[2,16,4,128]{3,2,1,0:T(4,128)S(1)}, u32[]{:S(2)}, u32[]{:S(2)}) collective-permute-start(f32[2,16,4,128]{3,2,1,0:T(4,128)S(1)} %get-tuple-element.27), channel_id=1, source_target_pairs={{1,0},{2,1},{3,2},{5,4},{6,5},{7,6},{9,8},{10,9},{11,10},{13,12},{... | collective-permute-start | bytes 196616 | tf_op jit(solution)/shard_map/ppermute | solution.py:20
  40.1 2.5 %collective-permute-start.3 = (f32[2,16,4,128]{3,2,1,0:T(4,128)S(1)}, f32[2,16,4,128]{3,2,1,0:T(4,128)S(1)}, u32[]{:S(2)}, u32[]{:S(2)}) collective-permute-start(f32[2,16,4,128]{3,2,1,0:T(4,128)S(1)} %get-tuple-element.26), channel_id=1, source_target_pairs={{0,1},{1,2},{2,3},{4,5},{5,6},{6,7},{8,9},{9,10},{10,11},{12,13},{... | collective-permute-start | bytes 196616 | tf_op jit(solution)/shard_map/ppermute | solution.py:18
  42.7 3.1 %collective-permute-done.3 = f32[2,16,4,128]{3,2,1,0:T(4,128)S(1)} collective-permute-done((f32[2,16,4,128]{3,2,1,0:T(4,128)S(1)}, f32[2,16,4,128]{3,2,1,0:T(4,128)S(1)}, u32[]{:S(2)}, u32[]{:S(2)}) %collective-permute-start.3) | collective-permute-done | bytes 65568 | tf_op jit(solution)/shard_map/ppermute | solution.py:18
  46.7 0.7 %fusion.18 = (f32[2,16,16,128]{3,2,1,0:T(8,128)S(1)}, f32[2,16,16,128]{3,2,1,0:T(8,128)S(1)}) fusion(f32[2,16,24,136]{3,2,1,0:T(8,128)S(1)} %select_maximum_fusion.5, f32[2,16,20,128]{3,2,1,0:T(8,128)S(1)} %get-tuple-element.25, f32[2,16,20,128]{3,2,1,0:T(8,128)S(1)} %get-tuple-element.24), kind=kLoop, calls=%fused_computation.48 | loop fusion | flops 1441792 | bytes 4718592 | tf_op jit(solution)/shard_map/add | solution.py:49
  47.4 0.6 fusion.101
  48.2 3.3 %collective-permute-start.7 = (f32[2,4,16,128]{3,2,1,0:T(8,128)S(1)}, f32[2,4,16,128]{3,2,1,0:T(8,128)S(1)}, u32[]{:S(2)}, u32[]{:S(2)}) collective-permute-start(f32[2,4,16,128]{3,2,1,0:T(8,128)S(1)} %get-tuple-element.33), channel_id=1, source_target_pairs={{4,0},{8,4},{12,8},{5,1},{9,5},{13,9},{6,2},{10,6},{14,10},{7,3},{... | collective-permute-start | bytes 196616 | tf_op jit(solution)/shard_map/ppermute | solution.py:20
  51.5 2.6 %collective-permute-start.8 = (f32[2,4,16,128]{3,2,1,0:T(8,128)S(1)}, f32[2,4,16,128]{3,2,1,0:T(8,128)S(1)}, u32[]{:S(2)}, u32[]{:S(2)}) collective-permute-start(f32[2,4,16,128]{3,2,1,0:T(8,128)S(1)} %get-tuple-element.32), channel_id=1, source_target_pairs={{0,4},{4,8},{8,12},{1,5},{5,9},{9,13},{2,6},{6,10},{10,14},{3,7},{... | collective-permute-start | bytes 196616 | tf_op jit(solution)/shard_map/ppermute | solution.py:18
  54.3 3.3 %collective-permute-done.8 = f32[2,4,16,128]{3,2,1,0:T(8,128)S(1)} collective-permute-done((f32[2,4,16,128]{3,2,1,0:T(8,128)S(1)}, f32[2,4,16,128]{3,2,1,0:T(8,128)S(1)}, u32[]{:S(2)}, u32[]{:S(2)}) %collective-permute-start.8) | collective-permute-done | bytes 65568 | tf_op jit(solution)/shard_map/ppermute | solution.py:18
  57.7 1.9 %collective-permute-start.9 = (f32[2,16,4,128]{3,2,1,0:T(4,128)S(1)}, f32[2,16,4,128]{3,2,1,0:T(4,128)S(1)}, u32[]{:S(2)}, u32[]{:S(2)}) collective-permute-start(f32[2,16,4,128]{3,2,1,0:T(4,128)S(1)} %get-tuple-element.23), channel_id=1, source_target_pairs={{1,0},{2,1},{3,2},{5,4},{6,5},{7,6},{9,8},{10,9},{11,10},{13,12},{... | collective-permute-start | bytes 196616 | tf_op jit(solution)/shard_map/ppermute | solution.py:20
  59.6 2.5 %collective-permute-start.10 = (f32[2,16,4,128]{3,2,1,0:T(4,128)S(1)}, f32[2,16,4,128]{3,2,1,0:T(4,128)S(1)}, u32[]{:S(2)}, u32[]{:S(2)}) collective-permute-start(f32[2,16,4,128]{3,2,1,0:T(4,128)S(1)} %get-tuple-element.22), channel_id=1, source_target_pairs={{0,1},{1,2},{2,3},{4,5},{5,6},{6,7},{8,9},{9,10},{10,11},{12,13},{... | collective-permute-start | bytes 196616 | tf_op jit(solution)/shard_map/ppermute | solution.py:18
  62.2 3.1 %collective-permute-done.10 = f32[2,16,4,128]{3,2,1,0:T(4,128)S(1)} collective-permute-done((f32[2,16,4,128]{3,2,1,0:T(4,128)S(1)}, f32[2,16,4,128]{3,2,1,0:T(4,128)S(1)}, u32[]{:S(2)}, u32[]{:S(2)}) %collective-permute-start.10) | collective-permute-done | bytes 65568 | tf_op jit(solution)/shard_map/ppermute | solution.py:18
  66.1 0.5 fusion.4
  67.0 0.6 fusion.50
  67.6 0.7 %fusion.155 = (f32[8,16,128]{2,1,0:T(8,128)}, f32[8,16,128]{2,1,0:T(8,128)}, f32[8,16,128]{2,1,0:T(8,128)S(1)}) fusion(f32[8,16,128]{2,1,0:T(8,128)S(1)} %add_add_fusion.3, bf16[2,8,16,128]{3,2,1,0:T(8,128)(2,1)S(1)} %copy-done.10, f32[8,16,128]{2,1,0:T(8,128)S(1)} %bitcast.73, f32[8,16,128]{2,1,0:T(8,128)S(1)} %copy-done.5, ...), kind=kLoop, calls=%fused_computation.279 | loop fusion | flops 327680 | bytes 983040 | tf_op jit(solution)/shard_map/add | solution.py:157
  68.3 0.7 add_add_fusion
  (65 shorter events, 4.1 us)
Async XLA Ops:
  0.6 4.5 %copy-start = (f32[1024,128]{1,0:T(8,128)S(1)}, f32[1024,128]{1,0:T(8,128)}, u32[]{:S(2)}) copy-start(f32[1024,128]{1,0:T(8,128)} %param.24) | copy-start | bytes 1572868
  6.9 12.6 %collective-permute-start.4 = (f32[3,1,64]{2,1,0:T(1,128)S(1)}, f32[3,1,64]{2,1,0:T(1,128)S(1)}, u32[]{:S(2)}, u32[]{:S(2)}) collective-permute-start(f32[3,1,64]{2,1,0:T(1,128)S(1)} %copy.28), channel_id=1, source_target_pairs={{0,4},{4,0},{8,12},{12,8},{1,5},{5,1},{9,13},{13,9},{2,6},{6,2},{1... | collective-permute-start | bytes 2312 | tf_op jit(solution)/shard_map/ppermute | solution.py:146
  7.4 12.2 %collective-permute-start.5 = (f32[3,1,64]{2,1,0:T(1,128)S(1)}, f32[3,1,64]{2,1,0:T(1,128)S(1)}, u32[]{:S(2)}, u32[]{:S(2)}) collective-permute-start(f32[3,1,64]{2,1,0:T(1,128)S(1)} %copy.29), channel_id=1, source_target_pairs={{0,8},{4,12},{8,0},{12,4},{1,9},{5,13},{9,1},{13,5},{2,10},{6,14},... | collective-permute-start | bytes 2312 | tf_op jit(solution)/shard_map/ppermute | solution.py:146
  10.1 9.5 %collective-permute-start.6 = (f32[3,1,64]{2,1,0:T(1,128)S(1)}, f32[3,1,64]{2,1,0:T(1,128)S(1)}, u32[]{:S(2)}, u32[]{:S(2)}) collective-permute-start(f32[3,1,64]{2,1,0:T(1,128)S(1)} %copy.30), channel_id=1, source_target_pairs={{0,12},{4,8},{8,4},{12,0},{1,13},{5,9},{9,5},{13,1},{2,14},{6,10},... | collective-permute-start | bytes 2312 | tf_op jit(solution)/shard_map/ppermute | solution.py:146
  11.4 26.6 %collective-permute-start = (f32[2,4,16,128]{3,2,1,0:T(8,128)S(1)}, f32[2,4,16,128]{3,2,1,0:T(8,128)S(1)}, u32[]{:S(2)}, u32[]{:S(2)}) collective-permute-start(f32[2,4,16,128]{3,2,1,0:T(8,128)S(1)} %get-tuple-element.42), channel_id=1, source_target_pairs={{4,0},{8,4},{12,8},{5,1},{9,5},{13,9},{6,2},{10,6},{14,10},{7,3},{... | collective-permute-start | bytes 196616 | tf_op jit(solution)/shard_map/ppermute | solution.py:20
  14.6 23.4 %collective-permute-start.1 = (f32[2,4,16,128]{3,2,1,0:T(8,128)S(1)}, f32[2,4,16,128]{3,2,1,0:T(8,128)S(1)}, u32[]{:S(2)}, u32[]{:S(2)}) collective-permute-start(f32[2,4,16,128]{3,2,1,0:T(8,128)S(1)} %get-tuple-element.41), channel_id=1, source_target_pairs={{0,4},{4,8},{8,12},{1,5},{5,9},{9,13},{2,6},{6,10},{10,14},{3,7},{... | collective-permute-start | bytes 196616 | tf_op jit(solution)/shard_map/ppermute | solution.py:18
  25.7 12.3 %copy-start.1 = (f32[8,16,128]{2,1,0:T(8,128)S(1)}, f32[8,16,128]{2,1,0:T(8,128)}, u32[]{:S(2)}) copy-start(f32[8,16,128]{2,1,0:T(8,128)} %param.15) | copy-start | bytes 196612
  25.7 12.3 %copy-start.3 = (f32[8,16,128]{2,1,0:T(8,128)S(1)}, f32[8,16,128]{2,1,0:T(8,128)}, u32[]{:S(2)}) copy-start(f32[8,16,128]{2,1,0:T(8,128)} %param.14) | copy-start | bytes 196612
  38.1 4.6 %collective-permute-start.2 = (f32[2,16,4,128]{3,2,1,0:T(4,128)S(1)}, f32[2,16,4,128]{3,2,1,0:T(4,128)S(1)}, u32[]{:S(2)}, u32[]{:S(2)}) collective-permute-start(f32[2,16,4,128]{3,2,1,0:T(4,128)S(1)} %get-tuple-element.27), channel_id=1, source_target_pairs={{1,0},{2,1},{3,2},{5,4},{6,5},{7,6},{9,8},{10,9},{11,10},{13,12},{... | collective-permute-start | bytes 196616 | tf_op jit(solution)/shard_map/ppermute | solution.py:20
  40.0 7.9 %copy-start.5 = (f32[8,16,128]{2,1,0:T(8,128)S(1)}, f32[8,16,128]{2,1,0:T(8,128)}, u32[]{:S(2)}) copy-start(f32[8,16,128]{2,1,0:T(8,128)} %param.18) | copy-start | bytes 196612
  40.0 7.9 %copy-start.6 = (f32[8,16,128]{2,1,0:T(8,128)S(1)}, f32[8,16,128]{2,1,0:T(8,128)}, u32[]{:S(2)}) copy-start(f32[8,16,128]{2,1,0:T(8,128)} %param.20) | copy-start | bytes 196612
  40.1 7.9 %copy-start.8 = (f32[8,16,128]{2,1,0:T(8,128)S(1)}, f32[8,16,128]{2,1,0:T(8,128)}, u32[]{:S(2)}) copy-start(f32[8,16,128]{2,1,0:T(8,128)} %param.17) | copy-start | bytes 196612
  40.1 5.7 %collective-permute-start.3 = (f32[2,16,4,128]{3,2,1,0:T(4,128)S(1)}, f32[2,16,4,128]{3,2,1,0:T(4,128)S(1)}, u32[]{:S(2)}, u32[]{:S(2)}) collective-permute-start(f32[2,16,4,128]{3,2,1,0:T(4,128)S(1)} %get-tuple-element.26), channel_id=1, source_target_pairs={{0,1},{1,2},{2,3},{4,5},{5,6},{6,7},{8,9},{9,10},{10,11},{12,13},{... | collective-permute-start | bytes 196616 | tf_op jit(solution)/shard_map/ppermute | solution.py:18
  42.6 5.4 %copy-start.7 = (f32[8,16,128]{2,1,0:T(8,128)S(1)}, f32[8,16,128]{2,1,0:T(8,128)}, u32[]{:S(2)}) copy-start(f32[8,16,128]{2,1,0:T(8,128)} %param.19) | copy-start | bytes 196612
  42.7 5.4 %copy-start.9 = (f32[8,16,128]{2,1,0:T(8,128)S(1)}, f32[8,16,128]{2,1,0:T(8,128)}, u32[]{:S(2)}) copy-start(f32[8,16,128]{2,1,0:T(8,128)} %param.16) | copy-start | bytes 196612
  48.0 20.2 %copy-start.2 = (f32[8,16,128]{2,1,0:T(8,128)}, f32[8,16,128]{2,1,0:T(8,128)S(1)}, u32[]{:S(2)}) copy-start(f32[8,16,128]{2,1,0:T(8,128)S(1)} %get-tuple-element.14) | copy-start | bytes 196612
  48.1 19.4 %copy-start.4 = (f32[8,16,128]{2,1,0:T(8,128)}, f32[8,16,128]{2,1,0:T(8,128)S(1)}, u32[]{:S(2)}) copy-start(f32[8,16,128]{2,1,0:T(8,128)S(1)} %add_add_fusion.3) | copy-start | bytes 196612
  48.2 6.2 %collective-permute-start.7 = (f32[2,4,16,128]{3,2,1,0:T(8,128)S(1)}, f32[2,4,16,128]{3,2,1,0:T(8,128)S(1)}, u32[]{:S(2)}, u32[]{:S(2)}) collective-permute-start(f32[2,4,16,128]{3,2,1,0:T(8,128)S(1)} %get-tuple-element.33), channel_id=1, source_target_pairs={{4,0},{8,4},{12,8},{5,1},{9,5},{13,9},{6,2},{10,6},{14,10},{7,3},{... | collective-permute-start | bytes 196616 | tf_op jit(solution)/shard_map/ppermute | solution.py:20
  51.5 6.2 %collective-permute-start.8 = (f32[2,4,16,128]{3,2,1,0:T(8,128)S(1)}, f32[2,4,16,128]{3,2,1,0:T(8,128)S(1)}, u32[]{:S(2)}, u32[]{:S(2)}) collective-permute-start(f32[2,4,16,128]{3,2,1,0:T(8,128)S(1)} %get-tuple-element.32), channel_id=1, source_target_pairs={{0,4},{4,8},{8,12},{1,5},{5,9},{9,13},{2,6},{6,10},{10,14},{3,7},{... | collective-permute-start | bytes 196616 | tf_op jit(solution)/shard_map/ppermute | solution.py:18
  57.7 4.5 %collective-permute-start.9 = (f32[2,16,4,128]{3,2,1,0:T(4,128)S(1)}, f32[2,16,4,128]{3,2,1,0:T(4,128)S(1)}, u32[]{:S(2)}, u32[]{:S(2)}) collective-permute-start(f32[2,16,4,128]{3,2,1,0:T(4,128)S(1)} %get-tuple-element.23), channel_id=1, source_target_pairs={{1,0},{2,1},{3,2},{5,4},{6,5},{7,6},{9,8},{10,9},{11,10},{13,12},{... | collective-permute-start | bytes 196616 | tf_op jit(solution)/shard_map/ppermute | solution.py:20
  59.6 8.0 %copy-start.10 = (bf16[2,8,16,128]{3,2,1,0:T(8,128)(2,1)S(1)}, bf16[2,8,16,128]{3,2,1,0:T(8,128)(2,1)}, u32[]{:S(2)}) copy-start(bf16[2,8,16,128]{3,2,1,0:T(8,128)(2,1)} %param.23) | copy-start | bytes 196612
  59.6 5.7 %collective-permute-start.10 = (f32[2,16,4,128]{3,2,1,0:T(4,128)S(1)}, f32[2,16,4,128]{3,2,1,0:T(4,128)S(1)}, u32[]{:S(2)}, u32[]{:S(2)}) collective-permute-start(f32[2,16,4,128]{3,2,1,0:T(4,128)S(1)} %get-tuple-element.22), channel_id=1, source_target_pairs={{0,1},{1,2},{2,3},{4,5},{5,6},{6,7},{8,9},{9,10},{10,11},{12,13},{... | collective-permute-start | bytes 196616 | tf_op jit(solution)/shard_map/ppermute | solution.py:18
